TPU v7x, 128 devices: a whole 4x4x4 slice. The times are simulated.
128 devices in a mesh: dp: 8 (over x, core), eig: 16 (over y, z).
Axes of the slice: x: 4, y: 4, z: 4, core: 2. Of those that a mesh axis runs over, the one named last changes fastest.
Arguments:
- acts: bfloat16 [4096, 8192], P(('dp', 'eig')), may hold values from -6 to 6
- grads: bfloat16 [4096, 8192], P(('dp', 'eig')), may hold values from -6 to 6
- act_basis: bfloat16 [4096, 8192], P('eig'), may hold values from -0.0625 to 0.0625
- grad_basis: bfloat16 [4096, 8192], P('eig'), may hold values from -0.0625 to 0.0625
- eigenvalues: float32 [4096, 4096], P('eig'), may hold values from 0.05 to 20
- query_grads: bfloat16 [32, 256, 4096], P('dp', None, 'eig'), may hold values from -6 to 6
- query_acts: bfloat16 [32, 256, 4096], P('dp'), may hold values from -6 to 6
- cand_local: int32 [8, 16], P('dp'), may hold values from 0 to 7, as said below
- seq_lengths: int32 [8, 8], P('dp'), may hold values from 1 to 128, 512 in all within a row
Outputs:
- scores: float32 [32, 16], P('dp')
Inputs may be any that keep to these rules, and one draw needn't show every extreme that they name: `cand_local`: entry j of an owner's list names a sequence of dp shard j // 2; the 2 entries of one list that name one shard differ. `seq_lengths`: row d lists the lengths of the 8 sequences packed in order in dp shard d's 512 token rows; they sum to 512.
All inputs are finite; a program needn't handle non-finite values.
Results may differ from a plain program's by a relative error of at most 0.006.
Values may be sent and summed in bfloat16 or wider, within the bound.
No kernel may reach another device: no remote copies, remote signals or barrier semaphores. Data moves between devices by JAX's collectives and lax.ppermute only.
A program may use at most 128 MiB of HBM per device.

v0:
```python
import math
import jax
import jax.numpy as jnp
from jax import lax
from jax.sharding import PartitionSpec as P

DAMPING = 0.1


def shards(
    acts,
    grads,
    act_basis,
    grad_basis,
    eigenvalues,
    query_grads,
    query_acts,
    cand_local,
    seq_lengths,
):
    block_width = act_basis.shape[0]
    stacked = jnp.stack([acts, grads])
    shard_rows = lax.all_gather(stacked, "eig", axis=1, tiled=True)
    act_part = jnp.dot(shard_rows[0], act_basis.T, preferred_element_type=jnp.float32)
    grad_part = jnp.dot(shard_rows[1], grad_basis.T, preferred_element_type=jnp.float32)
    rotated = jnp.concatenate([act_part, grad_part], axis=1).astype(jnp.bfloat16)
    act_block = rotated[:, :block_width]
    grad_block = rotated[:, block_width:]
    group_rows = rotated.shape[0]
    seq_count = seq_lengths.shape[1]
    max_len = 2 * group_rows // seq_count
    pick_lists = lax.all_to_all(cand_local, "dp", split_axis=1, concat_axis=0, tiled=True)
    owners = pick_lists.shape[0]
    per_shard = pick_lists.shape[1]
    lengths = seq_lengths[0]
    offsets = jnp.cumsum(lengths) - lengths
    chosen = (
        pick_lists[:, :, None] == jnp.arange(seq_count, dtype=jnp.int32)[None, None, :]
    ).astype(jnp.int32)
    pick_len = jnp.sum(chosen * lengths[None, None, :], axis=2)
    pick_start = jnp.sum(chosen * offsets[None, None, :], axis=2)
    within = jnp.arange(max_len, dtype=jnp.int32)
    is_live = within[None, None, :] < pick_len[:, :, None]
    row_index = jnp.where(is_live, pick_start[:, :, None] + within[None, None, :], 0).reshape(-1)
    live_rows = is_live.reshape(owners, per_shard * max_len, 1)

    def pack_rows(source):
        gathered_rows = jnp.take(source, row_index, axis=0).reshape(
            owners, per_shard * max_len, source.shape[1]
        )
        return jnp.where(live_rows, gathered_rows, jnp.zeros((), jnp.bfloat16))

    grad_pack = pack_rows(grad_block)
    grad_recv, act_narrow = (
        lax.all_to_all(grad_pack, "dp", split_axis=0, concat_axis=0, tiled=True),
        lax.all_to_all(pack_rows(act_block), "dp", split_axis=0, concat_axis=0, tiled=True),
    )
    act_recv = lax.all_gather(act_narrow, "eig", axis=2, tiled=True)
    slot_count = owners * per_shard * max_len
    full_width = query_acts.shape[2]
    grad_flat = grad_recv.reshape(slot_count, block_width).astype(jnp.float32)
    act_flat = act_recv.reshape(slot_count, full_width)
    damped = eigenvalues + DAMPING

    def score_query(query_pair):
        query_grad, query_act = query_pair
        query_outer = jnp.dot(query_grad.T, query_act, preferred_element_type=jnp.float32)
        precond = (query_outer / damped).astype(jnp.bfloat16)
        projected = lax.dot_general(
            act_flat, precond, (((1,), (1,)), ((), ())), preferred_element_type=jnp.float32
        )
        per_token = jnp.sum(projected * grad_flat, axis=1)
        return jnp.sum(per_token.reshape(owners * per_shard, max_len), axis=1)

    partial_sums = lax.map(score_query, (query_grads, query_acts))
    summed = lax.psum(partial_sums, "eig")
    score_scale = 1.0 / (full_width * 4.0 * math.sqrt(query_acts.shape[1]))
    return summed * score_scale


def solution(mesh):
    placed = (
        P(("dp", "eig"), None),
        P(("dp", "eig"), None),
        P("eig", None),
        P("eig", None),
        P("eig", None),
        P("dp", None, "eig"),
        P("dp", None, None),
        P("dp", None),
        P("dp", None),
    )
    return jax.shard_map(
        shards, mesh=mesh, in_specs=placed, out_specs=P("dp", None), check_vma=False
    )
```

profile of v0, /device:TPU:0, one launch (start us, length us, event | category | flops | bytes accessed | tf_op | source)
XLA Modules:
  0.0 384.3 jit_solution(13105366813927029866)
XLA Ops:
  6.5 2.3 pad_maximum_fusion
  8.9 0.5 broadcast.35
  9.4 1.3 reduce.3
  10.7 0.7 all_to_all.16
  11.4 4.4 %all-to-all-start = ((s32[1,8,2]{2,0,1:T(1,128)}), s32[1,8,2]{2,0,1:T(1,128)S(1)}, u32[]{:S(2)}, u32[]{:S(2)}) async-start(s32[1,8,2]{2,0,1:T(1,128)} %bitcast.6), calls=%async_computation | async-start | bytes 8192 | tf_op jit(solution)/shard_map/all_to_all | solution.py:32
  15.8 0.8 reduce-window.8
  16.7 0.7 bitcast_subtract_fusion
  17.3 3.7 all-to-all-done
  21.1 0.9 select_reduce_fusion.1
  22.3 101.1 %all-gather.3.cloned.1.call-done = bf16[2,512,8192]{2,1,0:T(8,128)(2,1)} async-done(((bf16[2,32,8192]{2,1,0:T(8,128)(2,1)}), bf16[2,512,8192]{2,1,0:T(8,128)(2,1)}) %all-gather.3.cloned.1.call-update) | async-done | bytes 16777232 | tf_op jit(solution)/shard_map/all_gather | solution.py:23
  123.4 6.9 %fusion.17 = bf16[512,256]{1,0:T(8,128)(2,1)S(1)} fusion(bf16[256,8192]{1,0:T(8,128)(2,1)} %param.15, bf16[2,512,8192]{2,1,0:T(8,128)(2,1)} %all-gather.3.cloned.1.call-done), kind=kOutput, calls=%fused_computation.18 | convolution fusion | flops 2147614720 | bytes 12845056 | tf_op jit(solution)/shard_map/dot_general | solution.py:24
  130.3 7.5 %gather_fusion = bf16[2048,256]{1,0:T(8,128)(2,1)S(1)} fusion(bf16[512,256]{1,0:T(8,128)(2,1)S(1)} %fusion.17, s32[2048]{0:T(1024)S(1)} %fusion.19), kind=kCustom, calls=%fused_computation.clone | custom fusion | bytes 2105344 | tf_op jit(solution)/shard_map/jit(_take)/gather | solution.py:48
  137.8 6.9 %fusion.18 = bf16[512,256]{1,0:T(8,128)(2,1)S(1)} fusion(bf16[256,8192]{1,0:T(8,128)(2,1)} %param.16, bf16[2,512,8192]{2,1,0:T(8,128)(2,1)} %all-gather.3.cloned.1.call-done), kind=kOutput, calls=%fused_computation.19 | convolution fusion | flops 2147614720 | bytes 12845056 | tf_op jit(solution)/shard_map/dot_general | solution.py:25
  144.8 7.5 %gather_fusion.1 = bf16[2048,256]{1,0:T(8,128)(2,1)S(1)} fusion(bf16[512,256]{1,0:T(8,128)(2,1)S(1)} %fusion.18, s32[2048]{0:T(1024)S(1)} %fusion.19), kind=kCustom, calls=%fused_computation.1.clone | custom fusion | bytes 2105344 | tf_op jit(solution)/shard_map/jit(_take)/gather | solution.py:48
  152.3 0.5 broadcast_select_fusion
  152.7 1.3 broadcast_select_fusion.2
  154.0 20.1 %all_to_all.23 = bf16[8,256,256]{2,1,0:T(8,128)(2,1)} all-to-all(bf16[8,256,256]{2,1,0:T(8,128)(2,1)S(1)} %get-tuple-element.63), channel_id=1, replica_groups=mesh['dp'=8,'eig'=16] {'dp'}, dimensions={0} | all-to-all | bytes 2097152 | tf_op jit(solution)/shard_map/all_to_all | solution.py:56
  174.2 3.6 all-to-all-start.2
  177.7 4.7 %broadcast_add_fusion = f32[256,4096]{1,0:T(8,128)} fusion(f32[256,4096]{1,0:T(8,128)} %param.17), kind=kLoop, calls=%fused_computation.17 | loop fusion | flops 1048576 | bytes 8388608 | tf_op jit(solution)/shard_map/add | solution.py:63
  182.5 11.1 %all-to-all-done.2 = bf16[8,256,256]{2,1,0:T(8,128)(2,1)S(1)} async-done(((bf16[8,256,256]{2,1,0:T(8,128)(2,1)}), bf16[8,256,256]{2,1,0:T(8,128)(2,1)S(1)}, u32[]{:S(2)}, u32[]{:S(2)}) %all-to-all-start.2) | async-done | bytes 1048608 | tf_op jit(solution)/shard_map/all_to_all | solution.py:55
  193.6 0.2 bitcast_convert_fusion
  193.8 1.9 copy.25
  195.7 96.4 %all-gather.5.cloned.1.call-done = bf16[8,256,4096]{2,1,0:T(8,128)(2,1)} async-done(((bf16[8,256,256]{2,1,0:T(8,128)(2,1)}), bf16[8,256,4096]{2,1,0:T(8,128)(2,1)}) %all-gather.5.cloned.1.call-update) | async-done | bytes 16777232 | tf_op jit(solution)/shard_map/all_gather | solution.py:58
  292.1 46.7 %while.10 = (s32[]{:T(128)}, f32[4,16]{1,0:T(4,128)S(1)}, bf16[4,256,256]{2,1,0:T(8,128)(2,1)}, bf16[4,256,4096]{2,1,0:T(8,128)(2,1)}, f32[256,4096]{1,0:T(8,128...) while((s32[]{:T(128)}, f32[4,16]{1,0:T(4,128)S(1)}, ...), condition=%wide.region_6.8_spmd, body=%wide.region_3.7_spmd.sunk | while | flops 4834983936 | bytes 25314592 | solution.py:75
  292.1 11.5 %fusion.30 = f32[2048]{0:T(1024)S(1)} fusion(f32[2048,256]{0,1:T(8,128)} %get-tuple-element.133, bf16[2048,4096]{1,0:T(8,128)(2,1)} %get-tuple-element.132, f32[256,4096]{1,0:T(8,128)} %get-tuple-element.131, bf16[4,256,4096]{2,1,0:T(8,128)(2,1)} %get-tuple-element.130, s32[]{:T(128)} %get-tuple-element.118, bf16[4,256,256]{2,1,0:T(8,128)(2,1)} %get-tuple-element.129), kind=kOutput, calls=%fused_computation.8.clone.1 | convolution fusion | flops 4834981888 | bytes 25306112 | tf_op jit(solution)/shard_map/while/body/eval_jaxpr/dot_general | solution.py:69
  303.6 0.1 bitcast_reduce_fusion.2
  303.7 11.5 %fusion.30 = f32[2048]{0:T(1024)S(1)} fusion(f32[2048,256]{0,1:T(8,128)} %get-tuple-element.133, bf16[2048,4096]{1,0:T(8,128)(2,1)} %get-tuple-element.132, f32[256,4096]{1,0:T(8,128)} %get-tuple-element.131, bf16[4,256,4096]{2,1,0:T(8,128)(2,1)} %get-tuple-element.130, s32[]{:T(128)} %get-tuple-element.118, bf16[4,256,256]{2,1,0:T(8,128)(2,1)} %get-tuple-element.129), kind=kOutput, calls=%fused_computation.8.clone.1 | convolution fusion | flops 4834981888 | bytes 25306112 | tf_op jit(solution)/shard_map/while/body/eval_jaxpr/dot_general | solution.py:69
  315.4 11.5 %fusion.30 = f32[2048]{0:T(1024)S(1)} fusion(f32[2048,256]{0,1:T(8,128)} %get-tuple-element.133, bf16[2048,4096]{1,0:T(8,128)(2,1)} %get-tuple-element.132, f32[256,4096]{1,0:T(8,128)} %get-tuple-element.131, bf16[4,256,4096]{2,1,0:T(8,128)(2,1)} %get-tuple-element.130, s32[]{:T(128)} %get-tuple-element.118, bf16[4,256,256]{2,1,0:T(8,128)(2,1)} %get-tuple-element.129), kind=kOutput, calls=%fused_computation.8.clone.1 | convolution fusion | flops 4834981888 | bytes 25306112 | tf_op jit(solution)/shard_map/while/body/eval_jaxpr/dot_general | solution.py:69
  326.9 0.1 bitcast_reduce_fusion.2
  327.1 11.5 %fusion.30 = f32[2048]{0:T(1024)S(1)} fusion(f32[2048,256]{0,1:T(8,128)} %get-tuple-element.133, bf16[2048,4096]{1,0:T(8,128)(2,1)} %get-tuple-element.132, f32[256,4096]{1,0:T(8,128)} %get-tuple-element.131, bf16[4,256,4096]{2,1,0:T(8,128)(2,1)} %get-tuple-element.130, s32[]{:T(128)} %get-tuple-element.118, bf16[4,256,256]{2,1,0:T(8,128)(2,1)} %get-tuple-element.129), kind=kOutput, calls=%fused_computation.8.clone.1 | convolution fusion | flops 4834981888 | bytes 25306112 | tf_op jit(solution)/shard_map/while/body/eval_jaxpr/dot_general | solution.py:69
  338.7 38.2 %psum.7 = f32[4,16]{1,0:T(4,128)S(1)} all-reduce(f32[4,16]{1,0:T(4,128)S(1)} %get-tuple-element.43), channel_id=1, replica_groups=mesh['dp'=8,'eig'=16] {'eig'}, use_global_device_ids=true, to_apply=%region_7.9 | all-reduce | flops 64 | bytes 512 | tf_op jit(solution)/shard_map/psum | solution.py:76
  376.9 0.6 broadcast_multiply_fusion
  (19 shorter events, 0.8 us)
Async XLA Ops:
  6.5 116.9 %all-gather.3.cloned.1.call-start = ((), (), s32[]{:S(2)}) async-start(), calls=%async_computation.3 | async-start | bytes 17825792 | tf_op jit(solution)/shard_map/all_gather | solution.py:23
  11.4 9.7 %all-to-all-start = ((s32[1,8,2]{2,0,1:T(1,128)}), s32[1,8,2]{2,0,1:T(1,128)S(1)}, u32[]{:S(2)}, u32[]{:S(2)}) async-start(s32[1,8,2]{2,0,1:T(1,128)} %bitcast.6), calls=%async_computation | async-start | bytes 8192 | tf_op jit(solution)/shard_map/all_to_all | solution.py:32
  15.8 276.3 %all-gather.5.cloned.1.call-start = ((), (), s32[]{:S(2)}) async-start(), calls=%async_computation.4 | async-start | bytes 17825792 | tf_op jit(solution)/shard_map/all_gather | solution.py:58
  174.2 19.4 %all-to-all-start.2 = ((bf16[8,256,256]{2,1,0:T(8,128)(2,1)}), bf16[8,256,256]{2,1,0:T(8,128)(2,1)S(1)}, u32[]{:S(2)}, u32[]{:S(2)}) async-start(bf16[8,256,256]{2,1,0:T(8,128)(2,1)} %get-tuple-element.62), calls=%async_computation.2 | async-start | bytes 2097152 | tf_op jit(solution)/shard_map/all_to_all | solution.py:55
Sparse Core Ops, SparseCore 0:
  9.5 113.8 all-gather.2
  174.3 117.7 all-gather.4
where the time goes:
time: 385 us; the launch traced here: 384 us
  waiting for transfers between devices  212 us (55%)
  matrix products  59.9 us (16%)
  blocking collectives  58.3 us (15%)
  local copies, waits for them, and re-layouts  18.4 us (5%)
  other arithmetic  13.8 us (4%)
  between operations  13.5 us (4%)
  starting transfers between devices  8.02 us (2%)
    all_gather x1, waiting for transfers between devices, shards(): shard_rows = lax.all_gather(stacked, 'eig', axis=1, tiled=True)  101 us
    all_gather x1, waiting for transfers between devices, shards(): act_recv = lax.all_gather(act_narrow, 'eig', axis=2, tiled=True)  96.4 us
    dot_general x4, matrix products, score_query(): lax.dot_general(act_flat, precond, (((1,), (1,)), ((), ())), preferred_el...  46 us
    psum x1, blocking collectives, shards(): summed = lax.psum(partial_sums, 'eig')  38.2 us
    all_to_all x1, blocking collectives, shards(): lax.all_to_all(pack_rows(act_block), 'dp', split_axis=0, concat_axis=0, t...  20.1 us
    gather x2, local copies, waits for them, and re-layouts, pack_rows(): jnp.take(source, row_index, axis=0)  15 us
    all_to_all x1, waiting for transfers between devices, shards(): lax.all_to_all(grad_pack, 'dp', split_axis=0, concat_axis=0, tiled=True)  11.1 us
  transfers between devices with their start and end apart: 4, of which 4 were waited for; matrix products, arithmetic and copies ran while one was open for 3% of the time, Pallas kernels for 0%

commit v1 on v0

--- a/solution.py
+++ b/solution.py
@@ -73,7 +73,7 @@
         return jnp.sum(per_token.reshape(owners * per_shard, max_len), axis=1)
 
     partial_sums = lax.map(score_query, (query_grads, query_acts))
-    summed = lax.psum(partial_sums, "eig")
+    summed = jnp.sum(lax.all_gather(partial_sums, "eig"), axis=0)
     score_scale = 1.0 / (full_width * 4.0 * math.sqrt(query_acts.shape[1]))
     return summed * score_scale
 

time: 385 us -> 369 us (0.958)
  blocking collectives: 58.3 us -> 42.9 us
    psum x1 -> x0, blocking collectives: 38.2 us -> none  [shards(): summed = lax.psum(partial_sums, 'eig')]
    all_gather x0 -> x1, blocking collectives: none -> 22.7 us  [shards(): summed = jnp.sum(lax.all_gather(partial_sums, 'eig'), axis=0)]
where the time goes in v1:
time: 369 us
  waiting for transfers between devices  212 us (57%)
  matrix products  59.9 us (16%)
  blocking collectives  42.9 us (12%)
  local copies, waits for them, and re-layouts  18.4 us (5%)
  other arithmetic  13.8 us (4%)
  between operations  13.5 us (4%)
  starting transfers between devices  8.02 us (2%)
    all_gather x1, waiting for transfers between devices, shards(): shard_rows = lax.all_gather(stacked, 'eig', axis=1, tiled=True)  101 us
    all_gather x1, waiting for transfers between devices, shards(): act_recv = lax.all_gather(act_narrow, 'eig', axis=2, tiled=True)  96.4 us
    dot_general x4, matrix products, score_query(): lax.dot_general(act_flat, precond, (((1,), (1,)), ((), ())), preferred_el...  46 us
    all_gather x1, blocking collectives, shards(): summed = jnp.sum(lax.all_gather(partial_sums, 'eig'), axis=0)  22.7 us
    all_to_all x1, blocking collectives, shards(): lax.all_to_all(pack_rows(act_block), 'dp', split_axis=0, concat_axis=0, t...  20.1 us
    gather x2, local copies, waits for them, and re-layouts, pack_rows(): jnp.take(source, row_index, axis=0)  15 us
    all_to_all x1, waiting for transfers between devices, shards(): lax.all_to_all(grad_pack, 'dp', split_axis=0, concat_axis=0, tiled=True)  11.1 us
  transfers between devices with their start and end apart: 4, of which 4 were waited for; matrix products, arithmetic and copies ran while one was open for 3% of the time, Pallas kernels for 0%

profile of v1, /device:TPU:0, one launch (start us, length us, event | category | flops | bytes accessed | tf_op | source)
XLA Modules:
  0.0 368.9 jit_solution(8878516603925922293)
XLA Ops:
  6.5 2.3 pad_maximum_fusion
  8.9 0.5 broadcast.35
  9.4 1.3 reduce.4
  10.7 0.7 all_to_all.16
  11.4 4.4 %all-to-all-start = ((s32[1,8,2]{2,0,1:T(1,128)}), s32[1,8,2]{2,0,1:T(1,128)S(1)}, u32[]{:S(2)}, u32[]{:S(2)}) async-start(s32[1,8,2]{2,0,1:T(1,128)} %bitcast.6), calls=%async_computation | async-start | bytes 8192 | tf_op jit(solution)/shard_map/all_to_all | solution.py:32
  15.8 0.8 reduce-window.8
  16.7 0.7 bitcast_subtract_fusion
  17.3 3.7 %all-to-all-done = s32[1,8,2]{2,0,1:T(1,128)S(1)} async-done(((s32[1,8,2]{2,0,1:T(1,128)}), s32[1,8,2]{2,0,1:T(1,128)S(1)}, u32[]{:S(2)}, u32[]{:S(2)}) %all-to-all-start) | async-done | bytes 96 | tf_op jit(solution)/shard_map/all_to_all | solution.py:32
  21.1 0.9 select_reduce_fusion.1
  22.3 101.1 %all-gather.5.cloned.1.call-done = bf16[2,512,8192]{2,1,0:T(8,128)(2,1)} async-done(((bf16[2,32,8192]{2,1,0:T(8,128)(2,1)}), bf16[2,512,8192]{2,1,0:T(8,128)(2,1)}) %all-gather.5.cloned.1.call-update) | async-done | bytes 16777232 | tf_op jit(solution)/shard_map/all_gather | solution.py:23
  123.4 6.9 %fusion.17 = bf16[512,256]{1,0:T(8,128)(2,1)S(1)} fusion(bf16[256,8192]{1,0:T(8,128)(2,1)} %param.15, bf16[2,512,8192]{2,1,0:T(8,128)(2,1)} %all-gather.5.cloned.1.call-done), kind=kOutput, calls=%fused_computation.18 | convolution fusion | flops 2147614720 | bytes 12845056 | tf_op jit(solution)/shard_map/dot_general | solution.py:24
  130.3 7.5 %gather_fusion = bf16[2048,256]{1,0:T(8,128)(2,1)S(1)} fusion(bf16[512,256]{1,0:T(8,128)(2,1)S(1)} %fusion.17, s32[2048]{0:T(1024)S(1)} %fusion.19), kind=kCustom, calls=%fused_computation.clone | custom fusion | bytes 2105344 | tf_op jit(solution)/shard_map/jit(_take)/gather | solution.py:48
  137.8 6.9 %fusion.18 = bf16[512,256]{1,0:T(8,128)(2,1)S(1)} fusion(bf16[256,8192]{1,0:T(8,128)(2,1)} %param.16, bf16[2,512,8192]{2,1,0:T(8,128)(2,1)} %all-gather.5.cloned.1.call-done), kind=kOutput, calls=%fused_computation.19 | convolution fusion | flops 2147614720 | bytes 12845056 | tf_op jit(solution)/shard_map/dot_general | solution.py:25
  144.8 7.5 %gather_fusion.1 = bf16[2048,256]{1,0:T(8,128)(2,1)S(1)} fusion(bf16[512,256]{1,0:T(8,128)(2,1)S(1)} %fusion.18, s32[2048]{0:T(1024)S(1)} %fusion.19), kind=kCustom, calls=%fused_computation.1.clone | custom fusion | bytes 2105344 | tf_op jit(solution)/shard_map/jit(_take)/gather | solution.py:48
  152.3 0.5 broadcast_select_fusion
  152.7 1.3 broadcast_select_fusion.2
  154.0 20.1 %all_to_all.23 = bf16[8,256,256]{2,1,0:T(8,128)(2,1)} all-to-all(bf16[8,256,256]{2,1,0:T(8,128)(2,1)S(1)} %get-tuple-element.63), channel_id=1, replica_groups=mesh['dp'=8,'eig'=16] {'dp'}, dimensions={0} | all-to-all | bytes 2097152 | tf_op jit(solution)/shard_map/all_to_all | solution.py:56
  174.2 3.6 all-to-all-start.2
  177.7 4.7 %broadcast_add_fusion = f32[256,4096]{1,0:T(8,128)} fusion(f32[256,4096]{1,0:T(8,128)} %param.17), kind=kLoop, calls=%fused_computation.17 | loop fusion | flops 1048576 | bytes 8388608 | tf_op jit(solution)/shard_map/add | solution.py:63
  182.5 11.1 %all-to-all-done.2 = bf16[8,256,256]{2,1,0:T(8,128)(2,1)S(1)} async-done(((bf16[8,256,256]{2,1,0:T(8,128)(2,1)}), bf16[8,256,256]{2,1,0:T(8,128)(2,1)S(1)}, u32[]{:S(2)}, u32[]{:S(2)}) %all-to-all-start.2) | async-done | bytes 1048608 | tf_op jit(solution)/shard_map/all_to_all | solution.py:55
  193.6 0.2 bitcast_convert_fusion
  193.8 1.9 copy.25
  195.7 96.4 %all-gather.7.cloned.1.call-done = bf16[8,256,4096]{2,1,0:T(8,128)(2,1)} async-done(((bf16[8,256,256]{2,1,0:T(8,128)(2,1)}), bf16[8,256,4096]{2,1,0:T(8,128)(2,1)}) %all-gather.7.cloned.1.call-update) | async-done | bytes 16777232 | tf_op jit(solution)/shard_map/all_gather | solution.py:58
  292.1 46.7 %while.10 = (s32[]{:T(128)}, f32[4,16]{1,0:T(4,128)S(1)}, bf16[4,256,256]{2,1,0:T(8,128)(2,1)}, bf16[4,256,4096]{2,1,0:T(8,128)(2,1)}, f32[256,4096]{1,0:T(8,128...) while((s32[]{:T(128)}, f32[4,16]{1,0:T(4,128)S(1)}, ...), condition=%wide.region_6.8_spmd, body=%wide.region_3.7_spmd.sunk | while | flops 4834983936 | bytes 25314592 | solution.py:75
  292.1 11.5 %fusion.30 = f32[2048]{0:T(1024)S(1)} fusion(f32[2048,256]{0,1:T(8,128)} %get-tuple-element.133, bf16[2048,4096]{1,0:T(8,128)(2,1)} %get-tuple-element.132, f32[256,4096]{1,0:T(8,128)} %get-tuple-element.131, bf16[4,256,4096]{2,1,0:T(8,128)(2,1)} %get-tuple-element.130, s32[]{:T(128)} %get-tuple-element.118, bf16[4,256,256]{2,1,0:T(8,128)(2,1)} %get-tuple-element.129), kind=kOutput, calls=%fused_computation.8.clone.1 | convolution fusion | flops 4834981888 | bytes 25306112 | tf_op jit(solution)/shard_map/while/body/eval_jaxpr/dot_general | solution.py:69
  303.6 0.1 bitcast_reduce_fusion.2
  303.7 11.5 %fusion.30 = f32[2048]{0:T(1024)S(1)} fusion(f32[2048,256]{0,1:T(8,128)} %get-tuple-element.133, bf16[2048,4096]{1,0:T(8,128)(2,1)} %get-tuple-element.132, f32[256,4096]{1,0:T(8,128)} %get-tuple-element.131, bf16[4,256,4096]{2,1,0:T(8,128)(2,1)} %get-tuple-element.130, s32[]{:T(128)} %get-tuple-element.118, bf16[4,256,256]{2,1,0:T(8,128)(2,1)} %get-tuple-element.129), kind=kOutput, calls=%fused_computation.8.clone.1 | convolution fusion | flops 4834981888 | bytes 25306112 | tf_op jit(solution)/shard_map/while/body/eval_jaxpr/dot_general | solution.py:69
  315.4 11.5 %fusion.30 = f32[2048]{0:T(1024)S(1)} fusion(f32[2048,256]{0,1:T(8,128)} %get-tuple-element.133, bf16[2048,4096]{1,0:T(8,128)(2,1)} %get-tuple-element.132, f32[256,4096]{1,0:T(8,128)} %get-tuple-element.131, bf16[4,256,4096]{2,1,0:T(8,128)(2,1)} %get-tuple-element.130, s32[]{:T(128)} %get-tuple-element.118, bf16[4,256,256]{2,1,0:T(8,128)(2,1)} %get-tuple-element.129), kind=kOutput, calls=%fused_computation.8.clone.1 | convolution fusion | flops 4834981888 | bytes 25306112 | tf_op jit(solution)/shard_map/while/body/eval_jaxpr/dot_general | solution.py:69
  326.9 0.1 bitcast_reduce_fusion.2
  327.1 11.5 %fusion.30 = f32[2048]{0:T(1024)S(1)} fusion(f32[2048,256]{0,1:T(8,128)} %get-tuple-element.133, bf16[2048,4096]{1,0:T(8,128)(2,1)} %get-tuple-element.132, f32[256,4096]{1,0:T(8,128)} %get-tuple-element.131, bf16[4,256,4096]{2,1,0:T(8,128)(2,1)} %get-tuple-element.130, s32[]{:T(128)} %get-tuple-element.118, bf16[4,256,256]{2,1,0:T(8,128)(2,1)} %get-tuple-element.129), kind=kOutput, calls=%fused_computation.8.clone.1 | convolution fusion | flops 4834981888 | bytes 25306112 | tf_op jit(solution)/shard_map/while/body/eval_jaxpr/dot_general | solution.py:69
  338.7 22.7 %all-gather.1 = f32[16,4,16]{2,1,0:T(4,128)S(1)} all-gather(f32[1,4,16]{2,1,0:T(4,128)S(1)} %bitcast.75), channel_id=2, replica_groups=mesh['dp'=8,'eig'=16] {'eig'}, dimensions={0}, use_global_device_ids=true | all-gather | bytes 4352 | tf_op jit(solution)/shard_map/all_gather | solution.py:76
  361.5 0.6 broadcast_multiply_fusion
  (20 shorter events, 0.8 us)
Async XLA Ops:
  6.5 116.9 %all-gather.5.cloned.1.call-start = ((), (), s32[]{:S(2)}) async-start(), calls=%async_computation.3 | async-start | bytes 17825792 | tf_op jit(solution)/shard_map/all_gather | solution.py:23
  11.4 9.7 %all-to-all-start = ((s32[1,8,2]{2,0,1:T(1,128)}), s32[1,8,2]{2,0,1:T(1,128)S(1)}, u32[]{:S(2)}, u32[]{:S(2)}) async-start(s32[1,8,2]{2,0,1:T(1,128)} %bitcast.6), calls=%async_computation | async-start | bytes 8192 | tf_op jit(solution)/shard_map/all_to_all | solution.py:32
  15.8 276.3 %all-gather.7.cloned.1.call-start = ((), (), s32[]{:S(2)}) async-start(), calls=%async_computation.4 | async-start | bytes 17825792 | tf_op jit(solution)/shard_map/all_gather | solution.py:58
  174.2 19.4 %all-to-all-start.2 = ((bf16[8,256,256]{2,1,0:T(8,128)(2,1)}), bf16[8,256,256]{2,1,0:T(8,128)(2,1)S(1)}, u32[]{:S(2)}, u32[]{:S(2)}) async-start(bf16[8,256,256]{2,1,0:T(8,128)(2,1)} %get-tuple-element.62), calls=%async_computation.2 | async-start | bytes 2097152 | tf_op jit(solution)/shard_map/all_to_all | solution.py:55
Sparse Core Ops, SparseCore 0:
  9.5 113.8 all-gather.4
  174.3 117.7 all-gather.6
